TPU v7x, 128 devices: a whole 4x4x4 slice. The times are simulated.
128 devices in a mesh: sec: 2 (over core), tile: 64 (over y, x, z).
Axes of the slice: x: 4, y: 4, z: 4, core: 2. Of those that a mesh axis runs over, the one named last changes fastest.
Arguments:
- land_wind: float32 [16384, 128], P(('sec', 'tile')), may hold values from 0.15 to 0.9
- land_moist: float32 [16384, 128], P(('sec', 'tile')), may hold values from 0 to 0.3
- texture: int32 [16384, 128], P(('sec', 'tile')), may hold values from 0 to 3
- land_index: int32 [16384, 128], P(('sec', 'tile')), may hold values from 0 to 32767
- erod_map: float32 [4194304], P(('sec', 'tile')), may hold values from 0.2 to 1
- mass_frac: float32 [4, 12], replicated, may hold values from 0.02 to 0.3
- blast_table: float32 [4, 8, 12], replicated, may hold values from 0.05 to 1
- dest_tile: int32 [16384, 1], P(('sec', 'tile')), may hold values from 0 to 127; in each aligned block of 128 rows (0 to 127, 128 to 255, ...) at most 2 rows name the same one
- regrid_w: bfloat16 [16384, 128, 256], P(('sec', 'tile')), may hold values from 0 to 0.25, as said below
- atm_state: float32 [3, 16, 32768], P(None, None, ('sec', 'tile')), may hold values from -5 to 5
- dust_mix: float32 [8, 16, 32768], P(None, None, ('sec', 'tile')), may hold values from 0 to 1
- mixing: float32 [15, 32768], P(None, ('sec', 'tile')), may hold values from 0.1 to 10
- settle: float32 [8], replicated, may hold values from 0.05 to 0.5
Outputs:
- land_fields: float32 [2, 16384, 128], P(None, ('sec', 'tile'))
- dust_out: float32 [8, 16, 32768], P(None, None, ('sec', 'tile'))
Inputs may be any that keep to these rules, and one draw needn't show every extreme that they name: `land_index`: each land cell's index points into its own device's 32768 cells of erod_map. `dest_tile`: among the 128 blocks of one device at most 2 name the same tile, a bound that some block reaches. `regrid_w`: each land cell has 1 to 4 positive weights, of 0.05 or more, on adjacent columns of its tile, and 0 elsewhere.
All inputs are finite; a program needn't handle non-finite values.
Results may differ from a plain program's by a relative error of at most 0.0023.
Values may be sent and summed in bfloat16 or wider, within the bound.
No kernel may reach another device: no remote copies, remote signals or barrier semaphores. Data moves between devices by JAX's collectives and lax.ppermute only.
A program may use at most 64 MiB of HBM per device.

v0:
```python
import jax
import jax.numpy as jnp
from jax import lax
from jax.sharding import PartitionSpec as P


def threshold_table(count):
    diameter = 4e-05 * jnp.power(jnp.float32(1.35), jnp.arange(count).astype(jnp.float32))
    return jnp.sqrt(0.0123 * (2160.0 * 9.81 * diameter + 0.0003 / (1.227 * diameter)))


def emit(wind_rows, moist_rows, texture_rows, erodible, mass_frac, blast_table, base_thresh):
    high = lax.Precision.HIGHEST
    thresh = base_thresh[:, None, None] * jnp.sqrt(1.0 + 12.1 * moist_rows)[None]
    classes = jnp.arange(mass_frac.shape[0])
    onehot = (texture_rows[None] == classes[:, None, None]).astype(jnp.float32)
    fraction = jnp.einsum("tb,tnl->bnl", mass_frac, onehot, precision=high)
    speed = wind_rows[None]
    salt = (
        40.0
        * fraction
        * erodible[None]
        * (speed + thresh)
        * jnp.maximum(speed * speed - thresh * thresh, 0.0)
    )
    blasted = jnp.einsum("tkb,bnl->tknl", blast_table, salt, precision=high)
    emission = jnp.sum(blasted * onehot[:, None], axis=0)
    return jnp.transpose(emission, (1, 0, 2)).astype(jnp.bfloat16)


def solve(right_side, coupling, sinking):
    levels = right_side.shape[1]
    sink_col = sinking[:, None]
    zero_row = jnp.zeros_like(coupling[0])
    ratios = []
    partial_value = []
    ratio_prev = None
    part_prev = None
    for level in range(levels):
        lower_c = coupling[level - 1] if level > 0 else zero_row
        upper_c = coupling[level] if level < levels - 1 else zero_row
        diagonal = 1.0 + lower_c[None] + upper_c[None] + sink_col
        if level == 0:
            pivot = diagonal
            part_now = right_side[:, level] / pivot
        else:
            pivot = diagonal + lower_c[None] * ratio_prev
            part_now = (right_side[:, level] + lower_c[None] * part_prev) / pivot
        if level < levels - 1:
            ratio_now = -(upper_c[None] + sink_col) / pivot
        else:
            ratio_now = jnp.zeros_like(pivot)
        ratios.append(ratio_now)
        partial_value.append(part_now)
        ratio_prev = ratio_now
        part_prev = part_now
    result = [None] * levels
    result[levels - 1] = partial_value[levels - 1]
    for level in range(levels - 2, -1, -1):
        result[level] = partial_value[level] - ratios[level] * result[level + 1]
    return jnp.stack(result, axis=1)


def on_device(
    land_wind,
    land_moist,
    texture,
    land_index,
    erod_map,
    mass_frac,
    blast_table,
    dest_tile,
    regrid_w,
    atm_state,
    dust_mix,
    mixing,
    settle,
):
    high = lax.Precision.HIGHEST
    nblocks, ncells = land_wind.shape
    columns = atm_state.shape[2]
    nbins = blast_table.shape[1]
    devices = lax.axis_size(("sec", "tile"))
    state = solve(atm_state, mixing, jnp.zeros((3,), jnp.float32))
    speed = jnp.sqrt(state[0, 0] ** 2 + state[1, 0] ** 2 + 0.25)
    surface = jnp.stack([speed, state[2, 0]]).astype(jnp.bfloat16).reshape(1, 2 * columns)
    gathered = lax.all_gather(surface, ("sec", "tile"), axis=0, tiled=True)
    base_thresh = threshold_table(mass_frac.shape[1])
    erodible = erod_map[land_index]
    emission = emit(land_wind, land_moist, texture, erodible, mass_frac, blast_table, base_thresh)
    partial_flux = jnp.einsum(
        "gkl,gla->gka", emission, regrid_w, preferred_element_type=jnp.float32
    )
    flat_flux = partial_flux.reshape(nblocks, nbins * columns)
    targets = dest_tile[:, 0]
    onehot = (targets[:, None] == jnp.arange(devices)[None, :]).astype(jnp.float32)
    capacity = max(2, 2 * nblocks // devices)
    before = jnp.cumsum(onehot, axis=0) - onehot
    ranking = jnp.sum(before * onehot, axis=1).astype(jnp.int32)
    slot_of = targets * capacity + ranking
    placing = (jnp.arange(devices * capacity)[:, None] == slot_of[None, :]).astype(jnp.float32)
    outgoing = jnp.dot(placing, flat_flux, precision=high).reshape(
        devices, capacity * nbins * columns
    )
    incoming = lax.all_to_all(
        outgoing.astype(jnp.bfloat16), ("sec", "tile"), split_axis=0, concat_axis=0, tiled=True
    ).astype(outgoing.dtype)
    flux = jnp.sum(incoming.reshape(devices * capacity, nbins, columns), axis=0)
    flux = flux * (float(columns) / float(ncells * nblocks))
    loaded = dust_mix.at[:, 0, :].add(flux)
    dust_out = solve(loaded, mixing, settle)
    picked = jnp.dot(onehot.astype(jnp.bfloat16), gathered, preferred_element_type=jnp.float32)
    picked = picked.astype(jnp.bfloat16).reshape(nblocks, 2, columns)
    numer = jnp.einsum("gla,gka->kgl", regrid_w, picked, preferred_element_type=jnp.float32)
    denom = jnp.sum(regrid_w, axis=2, dtype=jnp.float32)
    land_fields = jnp.stack([numer[0] / denom, 0.5 * land_moist + 0.5 * numer[1] / denom])
    return (land_fields, dust_out)


def solution(mesh):
    in_specs = (
        P(("sec", "tile"), None),
        P(("sec", "tile"), None),
        P(("sec", "tile"), None),
        P(("sec", "tile"), None),
        P(("sec", "tile")),
        P(),
        P(),
        P(("sec", "tile"), None),
        P(("sec", "tile"), None, None),
        P(None, None, ("sec", "tile")),
        P(None, None, ("sec", "tile")),
        P(None, ("sec", "tile")),
        P(),
    )
    out_specs = (P(None, ("sec", "tile"), None), P(None, None, ("sec", "tile")))
    return jax.shard_map(
        on_device, mesh=mesh, in_specs=in_specs, out_specs=out_specs, check_vma=False
    )
```

profile of v0, /device:TPU:1, one launch (start us, length us, event | category | flops | bytes accessed | tf_op | source)
XLA Modules:
  0.0 481.6 jit_solution(7172732893140782613)
XLA Ops:
  0.6 1.0 fusion.78
  1.7 1.0 broadcast_add_fusion.1
  2.7 0.9 fusion.79
  3.6 1.2 fusion.77
  4.9 0.1 multiply_add_fusion.15
  5.1 0.1 multiply_subtract_fusion.14
  5.4 321.0 %all-gather = bf16[128,1,512]{2,1,0:T(2,128)(2,1)S(1)} all-gather(bf16[1,1,512]{2,1,0:T(2,128)(2,1)S(1)} %reshape.27177), channel_id=1, replica_groups=mesh['sec'=2,'tile'=64] {'sec','tile'}, dimensions={0}, use_global_device_ids=true | all-gather | bytes 132096 | tf_op jit(solution)/shard_map/all_gather | solution.py:87
  326.4 0.7 fusion.17
  327.1 0.9 convolution_convert_fusion.1
  328.1 5.8 %convert_reduce_fusion = f32[128,128]{1,0:T(8,128)S(1)} fusion(bf16[128,128,256]{2,1,0:T(8,128)(2,1)} %param.23), kind=kLoop, calls=%fused_computation.1 | loop fusion | flops 8372224 | bytes 8454144 | tf_op jit(solution)/shard_map/reduce_sum | solution.py:115
  333.9 2.3 convolution_bitcast_fusion
  336.1 0.1 fusion.76
  336.3 90.5 %gather_fusion = f32[16384]{0:T(1024)S(1)} fusion(f32[32768]{0:T(1024)S(1)} %copy-done, s32[16384]{0:T(1024)S(1)} %fusion.15), kind=kCustom, calls=%fused_computation | custom fusion | bytes 196608 | tf_op jit(solution)/shard_map/gather | solution.py:89
  426.9 0.1 fusion.10
  427.1 0.8 fusion.4
  427.9 1.9 fusion
  429.8 4.6 fusion.7
  434.4 0.3 copy.136
  434.7 0.2 reduce_window_sum.11
  434.9 0.1 copy-done.31
  435.0 0.2 select_reduce_fusion
  435.2 1.0 convolution_convert_fusion
  436.2 1.9 convert_element_type.86
  438.2 0.5 broadcast.18933
  438.7 7.0 %reduce.4 = bf16[128,4096]{1,0:T(8,128)(2,1)S(1)} reduce(bf16[128,1,4096]{2,1,0:T(2,128)(2,1)S(1)} %convert_element_type.86, bf16[]{:T(256)} %broadcast.18933), dimensions={1}, to_apply=%convert_element_type.86.reduce_sub_computation | reduce | bytes 2097154 | tf_op jit(solution)/shard_map/convert_element_type | solution.py:106
  445.7 1.6 reshape.27184
  447.3 3.8 all-to-all-start
  451.1 0.7 pad_maximum_fusion
  451.8 0.1 fusion.75
  451.9 16.8 %all-to-all-done = bf16[128,2,2048]{2,1,0:T(2,128)(2,1)S(1)} async-done(((bf16[128,2,2048]{2,1,0:T(2,128)(2,1)}), bf16[128,2,2048]{2,1,0:T(2,128)(2,1)S(1)}, u32[]{:S(2)}, u32[]{:S(2)}) %all-to-all-start) | async-done | bytes 1048608 | tf_op jit(solution)/shard_map/all_to_all | solution.py:105
  468.7 1.0 reshape.27185
  469.7 7.5 %convert_reduce_fusion.1 = f32[128,4096]{1,0:T(8,128)} fusion(bf16[128,1,4096]{2,1,0:T(2,128)(2,1)S(1)} %reshape.27185), kind=kLoop, calls=%fused_computation.5 | loop fusion | flops 524288 | bytes 3145728 | tf_op jit(solution)/shard_map/convert_element_type | solution.py:107
  477.2 1.7 reshape.27164
  479.0 0.3 reduce_sum.42
  479.3 0.3 copy-done.7
  479.5 0.0 copy-done.9
  479.6 0.0 copy-done.11
  479.6 0.0 copy-done.23
  479.6 0.2 fusion.28
  479.8 0.2 constant_dynamic-update-slice_fusion.15
  480.0 0.1 constant_dynamic-update-slice_fusion.14
  480.1 0.1 constant_dynamic-update-slice_fusion.11
  480.3 0.1 constant_dynamic-update-slice_fusion.9
  480.4 0.1 constant_dynamic-update-slice_fusion.5
  480.5 0.1 constant_dynamic-update-slice_fusion.3
  480.7 0.1 constant_dynamic-update-slice_fusion.1
  480.8 0.1 constant_dynamic-update-slice_fusion
  480.9 0.7 copy.100
  (81 shorter events, 0.4 us)
Async XLA Ops:
  0.6 335.6 %copy-start = (f32[32768]{0:T(1024)S(1)}, f32[32768]{0:T(1024)}, u32[]{:S(2)}) copy-start(f32[32768]{0:T(1024)} %param.19) | copy-start | bytes 393220
  1.6 3.4 copy-start.14
  1.6 3.4 copy-start.16
  1.6 3.4 copy-start.18
  1.7 3.5 copy-start.24
  2.7 2.2 copy-start.8
  2.7 2.4 copy-start.10
  2.7 2.4 copy-start.12
  2.7 2.4 copy-start.20
  2.7 2.4 copy-start.22
  2.7 2.5 copy-start.27
  2.7 2.6 copy-start.29
  328.0 5.8 %copy-start.1 = (bf16[128,128,256]{2,1,0:T(8,128)(2,1)S(1)}, bf16[128,128,256]{2,1,0:T(8,128)(2,1)}, u32[]{:S(2)}) copy-start(bf16[128,128,256]{2,1,0:T(8,128)(2,1)} %param.23) | copy-start | bytes 25165828
  333.8 2.4 copy-start.6
  336.3 90.6 %copy-start.2 = (f32[128,128]{1,0:T(8,128)S(1)}, f32[128,128]{1,0:T(8,128)}, u32[]{:S(2)}) copy-start(f32[128,128]{1,0:T(8,128)} %param.15) | copy-start | bytes 196612
  336.3 90.6 %copy-start.5 = (s32[128,128]{1,0:T(8,128)S(1)}, s32[128,128]{1,0:T(8,128)}, u32[]{:S(2)}) copy-start(s32[128,128]{1,0:T(8,128)} %param.17) | copy-start | bytes 196612
  336.3 90.7 %copy-start.4 = (f32[128,128]{1,0:T(8,128)S(1)}, f32[128,128]{1,0:T(8,128)}, u32[]{:S(2)}) copy-start(f32[128,128]{1,0:T(8,128)} %param.16) | copy-start | bytes 196612
  336.3 90.7 %copy-start.32 = (f32[4,12]{1,0:T(4,128)S(1)}, f32[4,12]{1,0:T(4,128)}, u32[]{:S(2)}) copy-start(f32[4,12]{1,0:T(4,128)} %param.20) | copy-start | bytes 580
  426.9 1.0 copy-start.26
  434.4 0.7 copy-start.31
  445.7 6.1 %copy-start.3 = (f32[8,16,256]{2,1,0:T(8,128)S(1)}, f32[8,16,256]{2,1,0:T(8,128)}, u32[]{:S(2)}) copy-start(f32[8,16,256]{2,1,0:T(8,128)} %param.25) | copy-start | bytes 393220
  447.3 21.3 %all-to-all-start = ((bf16[128,2,2048]{2,1,0:T(2,128)(2,1)}), bf16[128,2,2048]{2,1,0:T(2,128)(2,1)S(1)}, u32[]{:S(2)}, u32[]{:S(2)}) async-start(bf16[128,2,2048]{2,1,0:T(2,128)(2,1)} %reshape.27184), calls=%async_computation | async-start | bytes 2097152 | tf_op jit(solution)/shard_map/all_to_all | solution.py:105
  478.9 0.7 copy-start.7
  478.9 0.7 copy-start.9
  478.9 0.7 copy-start.11
  478.9 0.7 copy-start.13
  478.9 0.7 copy-start.21
  478.9 0.7 copy-start.23
  478.9 0.7 copy-start.25
  479.0 0.7 copy-start.28
  479.0 0.7 copy-start.30
  479.0 0.8 copy-start.15
  479.0 0.8 copy-start.17
  479.0 0.8 copy-start.19
where the time goes:
time: 482 us
  blocking collectives  321 us (67%)
  local copies, waits for them, and re-layouts  101 us (21%)
  other arithmetic  26 us (5%)
  waiting for transfers between devices  16.8 us (3%)
  matrix products  11.4 us (2%)
    all_gather x1, blocking collectives, on_device(): gathered = lax.all_gather(surface, ('sec', 'tile'), axis=0, tiled=True)  321 us
    gather x1, local copies, waits for them, and re-layouts, on_device(): erodible = erod_map[land_index]  90.5 us
    all_to_all x1, waiting for transfers between devices, on_device(): lax.all_to_all(outgoing.astype(jnp.bfloat16), ('sec', 'tile'), split_axis...  16.8 us
  transfers between devices with their start and end apart: 1, of which 1 were waited for; matrix products, arithmetic and copies ran while one was open for 0% of the time, Pallas kernels for 0%

commit v1 on v0

--- a/solution.py
+++ b/solution.py
@@ -84,7 +84,10 @@
     state = solve(atm_state, mixing, jnp.zeros((3,), jnp.float32))
     speed = jnp.sqrt(state[0, 0] ** 2 + state[1, 0] ** 2 + 0.25)
     surface = jnp.stack([speed, state[2, 0]]).astype(jnp.bfloat16).reshape(1, 2 * columns)
-    gathered = lax.all_gather(surface, ("sec", "tile"), axis=0, tiled=True)
+    devices_2 = lax.axis_size(("sec", "tile"))
+    tiles = jnp.stack([surface for _ in range(devices_2)])
+    tiles = lax.all_to_all(tiles, ("sec", "tile"), split_axis=0, concat_axis=0)
+    gathered = jnp.concatenate(tiles, axis=0)
     base_thresh = threshold_table(mass_frac.shape[1])
     erodible = erod_map[land_index]
     emission = emit(land_wind, land_moist, texture, erodible, mass_frac, blast_table, base_thresh)

time: 482 us -> 184 us (0.38)
  blocking collectives: 321 us -> 0 us
  starting transfers between devices: 3.78 us -> 21.3 us
    all_gather x1 -> x0, blocking collectives: 321 us -> none  [on_device(): gathered = lax.all_gather(surface, ('sec', 'tile'), axis=0, tiled=True)]
    all_to_all x0 -> x1, starting transfers between devices: none -> 11.5 us  [on_device(): tiles = lax.all_to_all(tiles, ('sec', 'tile'), split_axis=0, concat_axis=0)]
    all_to_all x1, starting transfers between devices: 3.78 us -> 9.77 us  [on_device(): lax.all_to_all(outgoing.astype(jnp.bfloat16), ('sec', 'tile'), split_axis...]
  transfers between devices with their start and end apart: 1 -> 2, of which waited for: 1 -> 1; matrix products, arithmetic and copies ran while one was open for 0% -> 54% of each run, Pallas kernels for 0% -> 0%
where the time goes in v1:
time: 184 us; the launch traced here: 183 us
  local copies, waits for them, and re-layouts  103 us (56%)
  other arithmetic  26.6 us (14%)
  starting transfers between devices  21.3 us (12%)
  waiting for transfers between devices  16.3 us (9%)
  matrix products  14.1 us (8%)
  between operations  2.04 us (1%)
    gather x1, local copies, waits for them, and re-layouts, on_device(): erodible = erod_map[land_index]  90.5 us
    all_to_all x1, waiting for transfers between devices, on_device(): lax.all_to_all(outgoing.astype(jnp.bfloat16), ('sec', 'tile'), split_axis...  16.2 us
    all_to_all x1, starting transfers between devices, on_device(): tiles = lax.all_to_all(tiles, ('sec', 'tile'), split_axis=0, concat_axis=0)  11.5 us
    all_to_all x1, starting transfers between devices, on_device(): lax.all_to_all(outgoing.astype(jnp.bfloat16), ('sec', 'tile'), split_axis...  9.77 us
    convert_element_type x1, other arithmetic, on_device(): incoming = lax.all_to_all(outgoing.astype(jnp.bfloat16), ('sec', 'tile'),...  7.46 us
    convert_element_type x1, other arithmetic, on_device(): outgoing.astype(jnp.bfloat16)  7.03 us
    dot_general x1, matrix products, on_device(): jnp.einsum('gla,gka->kgl', regrid_w, picked, preferred_element_type=jnp.f...  5.66 us
    reduce_sum x1, other arithmetic, on_device(): denom = jnp.sum(regrid_w, axis=2, dtype=jnp.float32)  5.65 us
  transfers between devices with their start and end apart: 2, of which 1 were waited for; matrix products, arithmetic and copies ran while one was open for 54% of the time, Pallas kernels for 0%

profile of v1, /device:TPU:1, one launch (start us, length us, event | category | flops | bytes accessed | tf_op | source)
XLA Modules:
  0.0 183.0 jit_solution(8447883691844025357)
XLA Ops:
  0.6 1.0 fusion.78
  1.7 1.0 broadcast_add_fusion.1
  2.9 0.9 fusion.79
  3.8 1.2 fusion.77
  5.1 0.1 multiply_add_fusion.15
  5.2 0.1 multiply_subtract_fusion.14
  5.7 0.1 stack.12
  5.8 0.5 broadcast.18935
  6.3 1.4 reduce.4
  7.7 0.7 reshape.27182
  8.4 11.5 %all-to-all-start = ((bf16[128,2,256]{2,1,0:T(2,128)(2,1)}), bf16[128,2,256]{2,1,0:T(2,128)(2,1)S(1)}, u32[]{:S(2)}, u32[]{:S(2)}) async-start(bf16[128,2,256]{2,1,0:T(2,128)(2,1)} %reshape.27182), calls=%async_computation | async-start | bytes 262144 | tf_op jit(solution)/shard_map/all_to_all | solution.py:89
  19.9 5.6 %convert_reduce_fusion = f32[128,128]{1,0:T(8,128)S(1)} fusion(bf16[128,128,256]{2,1,0:T(8,128)(2,1)} %param.23), kind=kLoop, calls=%fused_computation.1 | loop fusion | flops 8372224 | bytes 8454144 | tf_op jit(solution)/shard_map/reduce_sum | solution.py:118
  25.7 90.5 %gather_fusion = f32[16384]{0:T(1024)S(1)} fusion(f32[32768]{0:T(1024)S(1)} %copy-done, s32[16384]{0:T(1024)S(1)} %fusion.15), kind=kCustom, calls=%fused_computation | custom fusion | bytes 196608 | tf_op jit(solution)/shard_map/gather | solution.py:92
  116.3 0.1 fusion.10
  116.4 0.1 fusion.17
  116.4 0.2 reduce_window_sum.11
  116.6 0.2 select_reduce_fusion
  116.9 0.1 reshape.27183
  117.0 0.2 convolution_convert_fusion.1
  117.3 5.7 %convolution_bitcast_fusion = f32[2,128,128]{2,0,1:T(2,128)S(1)} fusion(bf16[128,2,256]{2,1,0:T(2,128)(2,1)S(1)} %reshape.27163, bf16[128,128,256]{2,1,0:T(8,128)(2,1)} %param.23), kind=kOutput, calls=%fused_computation.14 | convolution fusion | flops 16777216 | bytes 8650752 | tf_op jit(solution)/shard_map/gla,gka->kgl/dot_general | solution.py:117
  122.9 0.1 fusion.76
  123.1 0.8 fusion.4
  124.0 1.8 fusion
  125.8 4.6 %fusion.7 = f32[128,8,256]{2,1,0:T(8,128)S(1)} fusion(bf16[128,128,256]{2,1,0:T(8,128)(2,1)} %param.23, bf16[8,128,128]{2,0,1:T(8,128)(2,1)S(1)} %fusion), kind=kOutput, calls=%fused_computation.17 | convolution fusion | flops 67108864 | bytes 9699328 | tf_op jit(solution)/shard_map/gkl,gla->gka/dot_general | solution.py:94
  130.3 0.3 copy.136
  130.7 1.0 convolution_convert_fusion
  131.7 1.9 %convert_element_type.84 = bf16[128,1,4096]{2,1,0:T(2,128)(2,1)S(1)} reshape(bf16[256,2048]{1,0:T(8,128)(2,1)S(1)} %convolution_convert_fusion) | data formatting | bytes 2097152 | tf_op jit(solution)/shard_map/convert_element_type | solution.py:109
  133.6 7.0 %reduce.5 = bf16[128,4096]{1,0:T(8,128)(2,1)S(1)} reduce(bf16[128,1,4096]{2,1,0:T(2,128)(2,1)S(1)} %convert_element_type.84, bf16[]{:T(256)} %broadcast.18935), dimensions={1}, to_apply=%convert_element_type.84.reduce_sub_computation | reduce | bytes 2097154 | tf_op jit(solution)/shard_map/convert_element_type | solution.py:109
  140.7 1.6 reshape.27184
  142.3 9.8 %all-to-all-start.1 = ((bf16[128,2,2048]{2,1,0:T(2,128)(2,1)}), bf16[128,2,2048]{2,1,0:T(2,128)(2,1)S(1)}, u32[]{:S(2)}, u32[]{:S(2)}) async-start(bf16[128,2,2048]{2,1,0:T(2,128)(2,1)} %reshape.27184), calls=%async_computation.1 | async-start | bytes 2097152 | tf_op jit(solution)/shard_map/all_to_all | solution.py:108
  152.1 0.7 fusion.75
  152.8 0.7 pad_maximum_fusion
  153.4 16.2 %all-to-all-done.1 = bf16[128,2,2048]{2,1,0:T(2,128)(2,1)S(1)} async-done(((bf16[128,2,2048]{2,1,0:T(2,128)(2,1)}), bf16[128,2,2048]{2,1,0:T(2,128)(2,1)S(1)}, u32[]{:S(2)}, u32[]{:S(2)}) %all-to-all-start.1) | async-done | bytes 1048608 | tf_op jit(solution)/shard_map/all_to_all | solution.py:108
  169.7 1.0 reshape.27185
  170.8 7.5 %convert_reduce_fusion.1 = f32[128,4096]{1,0:T(8,128)} fusion(bf16[128,1,4096]{2,1,0:T(2,128)(2,1)S(1)} %reshape.27185), kind=kLoop, calls=%fused_computation.5 | loop fusion | flops 524288 | bytes 3145728 | tf_op jit(solution)/shard_map/convert_element_type | solution.py:110
  178.2 1.7 reshape.27165
  180.3 0.3 reduce_sum.42
  180.6 0.0 copy-done.3
  180.9 0.2 fusion.28
  181.2 0.2 constant_dynamic-update-slice_fusion.15
  181.4 0.1 constant_dynamic-update-slice_fusion.14
  181.5 0.1 constant_dynamic-update-slice_fusion.11
  181.6 0.1 constant_dynamic-update-slice_fusion.9
  181.8 0.1 constant_dynamic-update-slice_fusion.5
  181.9 0.1 constant_dynamic-update-slice_fusion.3
  182.0 0.1 constant_dynamic-update-slice_fusion.1
  182.1 0.1 constant_dynamic-update-slice_fusion
  182.3 0.7 copy.99
  (170 shorter events, 0.7 us)
Async XLA Ops:
  0.6 25.0 %copy-start = (f32[32768]{0:T(1024)S(1)}, f32[32768]{0:T(1024)}, u32[]{:S(2)}) copy-start(f32[32768]{0:T(1024)} %param.19) | copy-start | bytes 393220
  1.6 3.8 %copy-start.17 = (f32[1,256]{1,0:T(1,128)}, f32[1,256]{1,0:T(1,128)S(1)}, u32[]{:S(2)}) copy-start(f32[1,256]{1,0:T(1,128)S(1)} %get-tuple-element.116) | copy-start | bytes 3076
  1.6 3.8 %copy-start.19 = (f32[1,256]{1,0:T(1,128)}, f32[1,256]{1,0:T(1,128)S(1)}, u32[]{:S(2)}) copy-start(f32[1,256]{1,0:T(1,128)S(1)} %get-tuple-element.117) | copy-start | bytes 3076
  1.6 3.8 %copy-start.27 = (f32[1,256]{1,0:T(1,128)}, f32[1,256]{1,0:T(1,128)S(1)}, u32[]{:S(2)}) copy-start(f32[1,256]{1,0:T(1,128)S(1)} %get-tuple-element.110) | copy-start | bytes 3076
  1.7 3.8 %copy-start.38 = (f32[1,256]{1,0:T(1,128)}, f32[1,256]{1,0:T(1,128)S(1)}, u32[]{:S(2)}) copy-start(f32[1,256]{1,0:T(1,128)S(1)} %get-tuple-element.111) | copy-start | bytes 3076
  1.7 3.8 %copy-start.40 = (f32[1,256]{1,0:T(1,128)}, f32[1,256]{1,0:T(1,128)S(1)}, u32[]{:S(2)}) copy-start(f32[1,256]{1,0:T(1,128)S(1)} %get-tuple-element.112) | copy-start | bytes 3076
  1.7 3.8 %copy-start.42 = (f32[1,256]{1,0:T(1,128)}, f32[1,256]{1,0:T(1,128)S(1)}, u32[]{:S(2)}) copy-start(f32[1,256]{1,0:T(1,128)S(1)} %get-tuple-element.122) | copy-start | bytes 3076
  1.7 3.8 %copy-start.56 = (f32[1,256]{1,0:T(1,128)}, f32[1,256]{1,0:T(1,128)S(1)}, u32[]{:S(2)}) copy-start(f32[1,256]{1,0:T(1,128)S(1)} %get-tuple-element.113) | copy-start | bytes 3076
  1.7 3.8 %copy-start.58 = (f32[1,256]{1,0:T(1,128)}, f32[1,256]{1,0:T(1,128)S(1)}, u32[]{:S(2)}) copy-start(f32[1,256]{1,0:T(1,128)S(1)} %get-tuple-element.114) | copy-start | bytes 3076
  1.7 3.8 %copy-start.60 = (f32[1,256]{1,0:T(1,128)}, f32[1,256]{1,0:T(1,128)S(1)}, u32[]{:S(2)}) copy-start(f32[1,256]{1,0:T(1,128)S(1)} %get-tuple-element.115) | copy-start | bytes 3076
  1.7 3.8 %copy-start.66 = (f32[1,256]{1,0:T(1,128)}, f32[1,256]{1,0:T(1,128)S(1)}, u32[]{:S(2)}) copy-start(f32[1,256]{1,0:T(1,128)S(1)} %get-tuple-element.121) | copy-start | bytes 3076
  1.7 23.9 %copy-start.4 = (f32[1,256]{1,0:T(1,128)}, f32[1,256]{1,0:T(1,128)S(1)}, u32[]{:S(2)}) copy-start(f32[1,256]{1,0:T(1,128)S(1)} %get-tuple-element.119) | copy-start | bytes 3076
  1.7 23.9 %copy-start.10 = (f32[1,256]{1,0:T(1,128)}, f32[1,256]{1,0:T(1,128)S(1)}, u32[]{:S(2)}) copy-start(f32[1,256]{1,0:T(1,128)S(1)} %get-tuple-element.109) | copy-start | bytes 3076
  2.8 2.5 %copy-start.71 = (f32[1,256]{1,0:T(1,128)}, f32[1,256]{1,0:T(1,128)S(1)}, u32[]{:S(2)}) copy-start(f32[1,256]{1,0:T(1,128)S(1)} %get-tuple-element.107) | copy-start | bytes 3076
  2.8 2.8 %copy-start.12 = (f32[1,256]{1,0:T(1,128)}, f32[1,256]{1,0:T(1,128)S(1)}, u32[]{:S(2)}) copy-start(f32[1,256]{1,0:T(1,128)S(1)} %get-tuple-element.99) | copy-start | bytes 3076
  2.8 2.8 %copy-start.29 = (f32[1,256]{1,0:T(1,128)}, f32[1,256]{1,0:T(1,128)S(1)}, u32[]{:S(2)}) copy-start(f32[1,256]{1,0:T(1,128)S(1)} %get-tuple-element.100) | copy-start | bytes 3076
  2.8 2.8 %copy-start.44 = (f32[1,256]{1,0:T(1,128)}, f32[1,256]{1,0:T(1,128)S(1)}, u32[]{:S(2)}) copy-start(f32[1,256]{1,0:T(1,128)S(1)} %get-tuple-element.101) | copy-start | bytes 3076
  2.8 2.8 %copy-start.46 = (f32[1,256]{1,0:T(1,128)}, f32[1,256]{1,0:T(1,128)S(1)}, u32[]{:S(2)}) copy-start(f32[1,256]{1,0:T(1,128)S(1)} %get-tuple-element.102) | copy-start | bytes 3076
  2.8 2.8 %copy-start.48 = (f32[1,256]{1,0:T(1,128)}, f32[1,256]{1,0:T(1,128)S(1)}, u32[]{:S(2)}) copy-start(f32[1,256]{1,0:T(1,128)S(1)} %get-tuple-element.103) | copy-start | bytes 3076
  2.8 2.8 %copy-start.62 = (f32[1,256]{1,0:T(1,128)}, f32[1,256]{1,0:T(1,128)S(1)}, u32[]{:S(2)}) copy-start(f32[1,256]{1,0:T(1,128)S(1)} %get-tuple-element.104) | copy-start | bytes 3076
  2.8 2.8 %copy-start.64 = (f32[1,256]{1,0:T(1,128)}, f32[1,256]{1,0:T(1,128)S(1)}, u32[]{:S(2)}) copy-start(f32[1,256]{1,0:T(1,128)S(1)} %get-tuple-element.105) | copy-start | bytes 3076
  2.8 2.8 %copy-start.69 = (f32[1,256]{1,0:T(1,128)}, f32[1,256]{1,0:T(1,128)S(1)}, u32[]{:S(2)}) copy-start(f32[1,256]{1,0:T(1,128)S(1)} %get-tuple-element.106) | copy-start | bytes 3076
  2.8 22.8 %copy-start.6 = (f32[1,256]{1,0:T(1,128)}, f32[1,256]{1,0:T(1,128)S(1)}, u32[]{:S(2)}) copy-start(f32[1,256]{1,0:T(1,128)S(1)} %get-tuple-element.108) | copy-start | bytes 3076
  3.7 1.9 %copy-start.21 = (f32[1,256]{1,0:T(1,128)}, f32[1,256]{1,0:T(1,128)S(1)}, u32[]{:S(2)}) copy-start(f32[1,256]{1,0:T(1,128)S(1)} %get-tuple-element.125) | copy-start | bytes 3076
  3.8 1.9 %copy-start.23 = (f32[1,256]{1,0:T(1,128)}, f32[1,256]{1,0:T(1,128)S(1)}, u32[]{:S(2)}) copy-start(f32[1,256]{1,0:T(1,128)S(1)} %get-tuple-element.126) | copy-start | bytes 3076
  3.8 1.9 %copy-start.25 = (f32[1,256]{1,0:T(1,128)}, f32[1,256]{1,0:T(1,128)S(1)}, u32[]{:S(2)}) copy-start(f32[1,256]{1,0:T(1,128)S(1)} %get-tuple-element.127) | copy-start | bytes 3076
  3.8 1.9 %copy-start.32 = (f32[1,256]{1,0:T(1,128)}, f32[1,256]{1,0:T(1,128)S(1)}, u32[]{:S(2)}) copy-start(f32[1,256]{1,0:T(1,128)S(1)} %get-tuple-element.128) | copy-start | bytes 3076
  3.8 1.9 %copy-start.34 = (f32[1,256]{1,0:T(1,128)}, f32[1,256]{1,0:T(1,128)S(1)}, u32[]{:S(2)}) copy-start(f32[1,256]{1,0:T(1,128)S(1)} %get-tuple-element.129) | copy-start | bytes 3076
  3.8 1.9 %copy-start.36 = (f32[1,256]{1,0:T(1,128)}, f32[1,256]{1,0:T(1,128)S(1)}, u32[]{:S(2)}) copy-start(f32[1,256]{1,0:T(1,128)S(1)} %get-tuple-element.124) | copy-start | bytes 3076
  3.8 21.8 %copy-start.8 = (f32[1,256]{1,0:T(1,128)}, f32[1,256]{1,0:T(1,128)S(1)}, u32[]{:S(2)}) copy-start(f32[1,256]{1,0:T(1,128)S(1)} %get-tuple-element.123) | copy-start | bytes 3076
  8.4 108.4 %all-to-all-start = ((bf16[128,2,256]{2,1,0:T(2,128)(2,1)}), bf16[128,2,256]{2,1,0:T(2,128)(2,1)S(1)}, u32[]{:S(2)}, u32[]{:S(2)}) async-start(bf16[128,2,256]{2,1,0:T(2,128)(2,1)} %reshape.27182), calls=%async_computation | async-start | bytes 262144 | tf_op jit(solution)/shard_map/all_to_all | solution.py:89
  19.9 5.7 %copy-start.16 = (s32[128,128]{1,0:T(8,128)S(1)}, s32[128,128]{1,0:T(8,128)}, u32[]{:S(2)}) copy-start(s32[128,128]{1,0:T(8,128)} %param.18) | copy-start | bytes 196612
  25.7 90.6 %copy-start.15 = (s32[128,128]{1,0:T(8,128)S(1)}, s32[128,128]{1,0:T(8,128)}, u32[]{:S(2)}) copy-start(s32[128,128]{1,0:T(8,128)} %param.17) | copy-start | bytes 196612
  25.7 90.7 %copy-start.73 = (s32[128,1]{0,1:T(1,128)S(1)}, s32[128,1]{0,1:T(1,128)}, u32[]{:S(2)}) copy-start(s32[128,1]{0,1:T(1,128)} %param.22) | copy-start | bytes 1540
  25.7 91.1 %copy-start.1 = (f32[128,128]{1,0:T(8,128)S(1)}, f32[128,128]{1,0:T(8,128)}, u32[]{:S(2)}) copy-start(f32[128,128]{1,0:T(8,128)} %param.15) | copy-start | bytes 196612
  117.2 5.8 %copy-start.14 = (f32[128,128]{1,0:T(8,128)S(1)}, f32[128,128]{1,0:T(8,128)}, u32[]{:S(2)}) copy-start(f32[128,128]{1,0:T(8,128)} %param.16) | copy-start | bytes 196612
  117.3 5.9 %copy-start.74 = (f32[4,12]{1,0:T(4,128)S(1)}, f32[4,12]{1,0:T(4,128)}, u32[]{:S(2)}) copy-start(f32[4,12]{1,0:T(4,128)} %param.20) | copy-start | bytes 580
  122.9 1.0 copy-start.68
  140.7 11.4 %copy-start.2 = (f32[8,16,256]{2,1,0:T(8,128)S(1)}, f32[8,16,256]{2,1,0:T(8,128)}, u32[]{:S(2)}) copy-start(f32[8,16,256]{2,1,0:T(8,128)} %param.25) | copy-start | bytes 393220
  142.3 27.4 %all-to-all-start.1 = ((bf16[128,2,2048]{2,1,0:T(2,128)(2,1)}), bf16[128,2,2048]{2,1,0:T(2,128)(2,1)S(1)}, u32[]{:S(2)}, u32[]{:S(2)}) async-start(bf16[128,2,2048]{2,1,0:T(2,128)(2,1)} %reshape.27184), calls=%async_computation.1 | async-start | bytes 2097152 | tf_op jit(solution)/shard_map/all_to_all | solution.py:108
  180.2 0.9 copy-start.5
  180.2 0.9 copy-start.18
  180.2 0.9 copy-start.20
  180.2 0.9 copy-start.28
  180.2 0.9 copy-start.33
  180.2 0.9 copy-start.35
  180.2 0.9 copy-start.39
  180.3 0.9 copy-start.41
  (29 other events, 20.7 us)
